TPU v7x, 32 devices: a whole 2x2x4 slice. The times are simulated.
32 devices in a mesh: row: 8 (over z, y), col: 4 (over x, core).
Axes of the slice: x: 2, y: 2, z: 4, core: 2. Of those that a mesh axis runs over, the one named last changes fastest.
Arguments:
- density: float32 [4, 256, 2048], P('col', 'row'), may hold values from 0.5 to 2
- momentum: float32 [3, 4, 256, 2048], P(None, 'col', 'row'), may hold values from -6 to 6
- energy: float32 [4, 256, 2048], P('col', 'row'), may hold values from 2 to 5
Outputs:
- tendency: float32 [5, 4, 256, 2048], P(None, 'col', 'row')
All inputs are finite; a program needn't handle non-finite values.
Results may differ from a plain program's by a relative error of at most 0.000053.
Values sent between devices are 32-bit elements; how exact they have to be, the bound alone decides.
No kernel may reach another device: no remote copies, remote signals or barrier semaphores. Data moves between devices by JAX's collectives and lax.ppermute only.
A program may use at most 64 MiB of HBM per device.

v0:
```python
import jax
import jax.numpy as jnp
import numpy as np
from jax import lax
from jax.sharding import PartitionSpec as P


def operator_column(count):
    steps = np.arange(count)
    wave = 2.0 * np.pi * steps / count
    upper = (
        17.0 / 12.0 * np.sin(wave)
        + 101.0 / 300.0 * np.sin(2.0 * wave)
        + 1.0 / 300.0 * np.sin(3.0 * wave)
    )
    lower = 1.0 + np.cos(wave) + 0.1 * np.cos(2.0 * wave)
    ratio = upper / lower
    phase = 2.0 * np.pi * (steps[:, None] * steps[None, :] % count) / count
    return -np.sum(ratio[:, None] * np.sin(phase), axis=0) / count


def operator_table(count):
    column = operator_column(count)
    steps = np.arange(count)
    offsets = (steps[None, :] - steps[:, None]) % count
    return column[offsets].astype(np.float32)


def block_weights(count):
    table = operator_table(count)
    width = 128
    w_self = table[:width, :width]
    w_prev = table[:width, width : 2 * width]
    w_next = table[width : 2 * width, :width]
    return jnp.asarray(np.concatenate([w_prev, w_self, w_next], axis=1))


def compact_last(field):
    count = field.shape[-1]
    width = 128
    blocks = field.reshape(field.shape[:-1] + (count // width, width))
    parts = jnp.einsum(
        "...bj,jk->...bk", blocks, block_weights(count), precision=lax.Precision.HIGHEST
    )
    result = (
        jnp.roll(parts[..., :width], 1, axis=-2)
        + parts[..., width : 2 * width]
        + jnp.roll(parts[..., 2 * width :], -1, axis=-2)
    )
    return result.reshape(field.shape)


def compact_second(field):
    count = field.shape[-2]
    if count <= 256:
        weights = jnp.asarray(operator_table(count))
        return jnp.einsum("...jc,ji->...ic", field, weights, precision=lax.Precision.HIGHEST)
    width = 128
    blocks = field.reshape(field.shape[:-2] + (count // width, width, field.shape[-1]))
    parts = jnp.einsum(
        "...bjc,jk->...bkc", blocks, block_weights(count), precision=lax.Precision.HIGHEST
    )
    result = (
        jnp.roll(parts[..., :width, :], 1, axis=-3)
        + parts[..., width : 2 * width, :]
        + jnp.roll(parts[..., 2 * width :, :], -1, axis=-3)
    )
    return result.reshape(field.shape)


def fluxes(density, momentum, energy):
    speed = momentum / density[None]
    pressure = 0.4 * (energy - 0.5 * jnp.sum(momentum * momentum, axis=0) / density)
    enthalpy = energy + pressure
    vel_x, vel_y = (speed[0], speed[1])
    flux_x = jnp.stack(
        [
            momentum[0],
            momentum[0] * vel_x + pressure,
            momentum[1] * vel_x,
            momentum[2] * vel_x,
            enthalpy * vel_x,
        ]
    )
    flux_y = jnp.stack(
        [
            momentum[1],
            momentum[0] * vel_y,
            momentum[1] * vel_y + pressure,
            momentum[2] * vel_y,
            enthalpy * vel_y,
        ],
        axis=2,
    )
    return (flux_x, flux_y)


def local(density, momentum, energy):
    flux_x, flux_y = fluxes(density, momentum, energy)
    planes, owned, length = (flux_y.shape[0], flux_y.shape[1], flux_y.shape[3])
    packed = flux_y.reshape(planes, owned, 5 * length)
    derivative_x = compact_last(flux_x)
    y_lines = lax.all_to_all(packed, "row", split_axis=2, concat_axis=1, tiled=True)
    derivative_lines = compact_second(y_lines)
    derived = lax.all_to_all(derivative_lines, "row", split_axis=1, concat_axis=2, tiled=True)
    derivative_y = jnp.transpose(derived.reshape(planes, owned, 5, length), (2, 0, 1, 3))
    return -(derivative_x + derivative_y)


def solution(mesh):
    in_specs = (P("col", "row", None), P(None, "col", "row", None), P("col", "row", None))
    out_specs = P(None, "col", "row", None)
    return jax.shard_map(local, mesh=mesh, in_specs=in_specs, out_specs=out_specs, check_vma=False)
```

profile of v0, /device:TPU:0, one launch (start us, length us, event | category | flops | bytes accessed | tf_op | source)
XLA Modules:
  0.0 174.0 jit_solution(4821467168655819884)
XLA Ops:
  0.0 0.0 copy-start
  0.0 1.0 bitcast_dynamic-update-slice_fusion.9
  1.0 0.0 copy-start.1
  1.1 0.0 copy-start.2
  1.1 1.4 multiply_reduce_fusion
  2.5 0.0 copy-done
  2.5 0.0 copy-done.1
  2.5 0.0 copy-done.2
  2.5 0.1 bitcast_dynamic-update-slice_fusion.7
  2.7 3.8 %copy.31 = f32[1,32,5,2048]{1,3,2,0:T(8,128)} copy(f32[1,32,5,2048]{3,1,2,0:T(8,128)S(1)} %bitcast_dynamic-update-slice_fusion.5) | data formatting | bytes 2621440 | tf_op jit(solution)/shard_map/reshape | solution.py:101
  6.5 0.5 broadcast.11
  7.0 47.4 %reduce.1 = f32[10240,32]{1,0:T(8,128)} reduce(f32[10240,1,32]{2,1,0:T(1,128)} %bitcast.106, f32[]{:T(128)} %broadcast.11), dimensions={1}, to_apply=%bitcast.93.reduce_sub_computation | reduce | bytes 2621444
  54.4 5.3 %reshape.146 = f32[8,1,40960]{2,1,0:T(1,128)} reshape(f32[10240,32]{1,0:T(8,128)} %reduce.1) | data formatting | bytes 2621440
  59.8 38.7 %all_to_all.30 = f32[8,1,40960]{2,1,0:T(1,128)S(1)} all-to-all(f32[8,1,40960]{2,1,0:T(1,128)} %reshape.146), channel_id=1, replica_groups=mesh['row'=8,'col'=4] {'row'}, dimensions={0} | all-to-all | bytes 2621440 | tf_op jit(solution)/shard_map/all_to_all | solution.py:103
  98.4 5.2 %reduce.2 = f32[8,40960]{1,0:T(8,128)} reduce(f32[8,1,40960]{2,1,0:T(1,128)S(1)} %all_to_all.30, f32[]{:T(128)} %broadcast.11), dimensions={1}, to_apply=%all_to_all.22.reduce_sub_computation | reduce | bytes 2621444 | tf_op jit(solution)/shard_map/all_to_all | solution.py:103
  103.7 12.0 %reshape.147 = f32[10240,1,32]{2,1,0:T(1,128)} reshape(f32[8,40960]{1,0:T(8,128)} %reduce.2) | data formatting | bytes 2621440
  115.6 10.6 %copy.26 = f32[1,32,10240]{2,1,0:T(8,128)} copy(f32[1,32,10240]{1,0,2:T(1,128)} %bitcast.107) | data formatting | bytes 2621440 | tf_op jit(solution)/shard_map/all_to_all | solution.py:103
  126.2 1.5 reshape.141
  127.8 2.2 %convolution_bitcast_fusion = f32[1,256,1280]{2,1,0:T(8,128)S(1)} fusion(f32[256,256]{1,0:T(8,128)} %constant.17, f32[256,1280]{1,0:T(8,128)S(1)} %reshape.141), kind=kOutput, calls=%fused_computation | convolution fusion | flops 1006632960 | bytes 2883584 | tf_op jit(solution)/shard_map/...jc,ji->...ic/dot_general | solution.py:57
  130.0 2.4 %copy.27 = f32[1,256,1280]{2,0,1:T(1,128)} copy(f32[1,256,1280]{2,1,0:T(8,128)S(1)} %convolution_bitcast_fusion) | data formatting | bytes 2621440 | tf_op jit(solution)/shard_map/...jc,ji->...ic/transpose | solution.py:57
  132.4 4.3 %all-to-all-start.1 = ((f32[1,256,1280]{2,0,1:T(1,128)}), f32[1,256,1280]{2,0,1:T(1,128)}, u32[]{:S(2)}, u32[]{:S(2)}) async-start(f32[1,256,1280]{2,0,1:T(1,128)} %copy.27), calls=%async_computation.1 | async-start | bytes 2621440 | tf_op jit(solution)/shard_map/all_to_all | solution.py:105
  136.6 0.1 multiply_bitcast_fusion
  136.9 0.1 fusion.7
  137.1 0.0 copy-start.3
  137.2 0.8 copy-done.3
  138.0 3.5 %convolution_bitcast_fusion.1 = f32[5,1,32,16,384]{4,3,2,0,1:T(8,128)S(1)} fusion(f32[5,32,16,128]{3,2,1,0:T(8,128)S(1)} %bitcast_dynamic-update-slice_fusion, f32[128,384,1,1]{1,0,3,2:T(8,128)S(1)} %copy-done.3), kind=kOutput, calls=%fused_computation.1 | convolution fusion | flops 1509949440 | bytes 5439488 | tf_op jit(solution)/shard_map/...bj,jk->...bk/dot_general | solution.py:42
  141.5 0.1 fusion.10
  141.6 0.2 fusion.9
  141.9 0.4 fusion
  142.2 0.2 reshape.137
  142.4 24.9 %all-to-all-done.1 = f32[1,256,1280]{2,0,1:T(1,128)} async-done(((f32[1,256,1280]{2,0,1:T(1,128)}), f32[1,256,1280]{2,0,1:T(1,128)}, u32[]{:S(2)}, u32[]{:S(2)}) %all-to-all-start.1) | async-done | bytes 1310752 | tf_op jit(solution)/shard_map/all_to_all | solution.py:105
  167.3 3.1 %copy.40 = f32[1,8,32,1280]{3,1,2,0:T(8,128)} copy(f32[1,8,32,1280]{3,0,2,1:T(1,128)} %bitcast.16) | data formatting | bytes 2621440 | tf_op jit(solution)/shard_map/all_to_all | solution.py:105
  170.5 1.5 reshape.140
  172.0 2.0 %fusion.1 = f32[5,1,32,2048]{3,2,1,0:T(8,128)} fusion(f32[5,1,32,2048]{3,2,1,0:T(8,128)S(1)} %reshape.137, f32[1,32,5,2048]{3,2,1,0:T(8,128)S(1)} %reshape.140), kind=kLoop, calls=%fused_computation.5 | loop fusion | flops 655360 | bytes 3932160 | tf_op jit(solution)/shard_map/neg | solution.py:107
  (13 shorter events, 0.4 us)
Async XLA Ops:
  0.0 2.5 %copy-start = (f32[3,1,32,2048]{3,2,1,0:T(8,128)S(1)}, f32[3,1,32,2048]{3,2,1,0:T(8,128)}, u32[]{:S(2)}) copy-start(f32[3,1,32,2048]{3,2,1,0:T(8,128)} %param.6) | copy-start | bytes 2359300
  1.0 1.5 copy-start.1
  1.1 1.5 copy-start.2
  132.4 35.0 %all-to-all-start.1 = ((f32[1,256,1280]{2,0,1:T(1,128)}), f32[1,256,1280]{2,0,1:T(1,128)}, u32[]{:S(2)}, u32[]{:S(2)}) async-start(f32[1,256,1280]{2,0,1:T(1,128)} %copy.27), calls=%async_computation.1 | async-start | bytes 2621440 | tf_op jit(solution)/shard_map/all_to_all | solution.py:105
  137.1 0.9 copy-start.3
where the time goes:
time: 175 us; the launch traced here: 174 us
  other arithmetic  56.7 us (32%)
  local copies, waits for them, and re-layouts  43.5 us (25%)
  blocking collectives  38.7 us (22%)
  waiting for transfers between devices  24.9 us (14%)
  matrix products  5.71 us (3%)
  starting transfers between devices  4.26 us (2%)
    unnamed x6, other arithmetic  47.7 us
    all_to_all x1, blocking collectives, local(): lax.all_to_all(packed, 'row', split_axis=2, concat_axis=1, tiled=True)  38.7 us
    all_to_all x1, waiting for transfers between devices, local(): lax.all_to_all(derivative_lines, 'row', split_axis=1, concat_axis=2, tile...  24.9 us
    unnamed x21, local copies, waits for them, and re-layouts  20 us
    all_to_all x1, local copies, waits for them, and re-layouts, local(): lax.all_to_all(packed, 'row', split_axis=2, concat_axis=1, tiled=True)  10.6 us
    all_to_all x1, other arithmetic, local(): lax.all_to_all(packed, 'row', split_axis=2, concat_axis=1, tiled=True)  5.24 us
    all_to_all x1, starting transfers between devices, local(): lax.all_to_all(derivative_lines, 'row', split_axis=1, concat_axis=2, tile...  4.26 us
    reshape x1, local copies, waits for them, and re-layouts, local(): packed = flux_y.reshape(planes, owned, 5 * length)  3.76 us
  transfers between devices with their start and end apart: 1, of which 1 were waited for; matrix products, arithmetic and copies ran while one was open for 3% of the time, Pallas kernels for 0%

commit v1 on v0

--- a/solution.py
+++ b/solution.py
@@ -3,6 +3,28 @@
 import numpy as np
 from jax import lax
 from jax.sharding import PartitionSpec as P
+
+
+def in_blocks(value, dim, size):
+    before, after = (value.shape[:dim], value.shape[dim + 1 :])
+    return jnp.moveaxis(value.reshape(*before, size, -1, *after), dim, 0)
+
+
+def in_order(parts, dim):
+    parts = jnp.moveaxis(parts, 0, dim)
+    dims = parts.shape
+    return parts.reshape(*dims[:dim], dims[dim] * dims[dim + 1], *dims[dim + 2 :])
+
+
+def pairwise_exchange(x, axis, split_dim, concat_dim):
+    size, here = (lax.axis_size(axis), lax.axis_index(axis))
+    parts = in_blocks(x, split_dim, size)
+    done = [parts[here]]
+    for step in range(1, size):
+        sent = parts[here ^ step]
+        done.append(lax.ppermute(sent, axis, [(i, i ^ step) for i in range(size)]))
+    parts = jnp.stack(done)[here ^ jnp.arange(size)]
+    return in_order(parts, concat_dim)
 
 
 def operator_column(count):
@@ -102,7 +124,7 @@
     derivative_x = compact_last(flux_x)
     y_lines = lax.all_to_all(packed, "row", split_axis=2, concat_axis=1, tiled=True)
     derivative_lines = compact_second(y_lines)
-    derived = lax.all_to_all(derivative_lines, "row", split_axis=1, concat_axis=2, tiled=True)
+    derived = pairwise_exchange(derivative_lines, "row", 1, 2)
     derivative_y = jnp.transpose(derived.reshape(planes, owned, 5, length), (2, 0, 1, 3))
     return -(derivative_x + derivative_y)
 

time: 175 us -> 166 us (0.949)
  blocking collectives: 38.7 us -> 0 us
  waiting for transfers between devices: 24.9 us -> 41.1 us
  starting transfers between devices: 4.26 us -> 17.3 us
    all_to_all x1 -> x0, blocking collectives: 38.7 us -> none  [local(): lax.all_to_all(packed, 'row', split_axis=2, concat_axis=1, tiled=True)]
    ppermute x0 -> x7, waiting for transfers between devices: none -> 16.4 us  [pairwise_exchange(): done.append(lax.ppermute(sent, axis, [(i, i ^ step) for i in range(size)]))]
    ppermute x0 -> x7, starting transfers between devices: none -> 10 us  [pairwise_exchange(): done.append(lax.ppermute(sent, axis, [(i, i ^ step) for i in range(size)]))]
    unnamed x21 -> x31, local copies, waits for them, and re-layouts: 20 us -> 24.6 us
    all_to_all x1 -> x0, local copies, waits for them, and re-layouts: 3.13 us -> none  [local(): lax.all_to_all(derivative_lines, 'row', split_axis=1, concat_axis=2, tile...]
    all_to_all x1, starting transfers between devices: 4.26 us -> 7.28 us  [local(): lax.all_to_all(packed, 'row', split_axis=2, concat_axis=1, tiled=True)]
    another operation x0 -> x2, local copies, waits for them, and re-layouts: none -> 2.23 us  [the longest x1 1.54 us: local(): derived.reshape(planes, owned, 5, length)]
    gather x0 -> x1, local copies, waits for them, and re-layouts: none -> 1.95 us  [pairwise_exchange(): parts = jnp.stack(done)[here ^ jnp.arange(size)]]
  transfers between devices with their start and end apart: 1 -> 8, of which waited for: 1 -> 4; matrix products, arithmetic and copies ran while one was open for 3% -> 7% of each run, Pallas kernels for 0% -> 0%
where the time goes in v1:
time: 166 us; the launch traced here: 165 us
  other arithmetic  56.1 us (34%)
  local copies, waits for them, and re-layouts  45.1 us (27%)
  waiting for transfers between devices  41.1 us (25%)
  starting transfers between devices  17.3 us (10%)
  matrix products  4.74 us (3%)
    unnamed x6, other arithmetic  47.6 us
    all_to_all x1, waiting for transfers between devices, local(): lax.all_to_all(packed, 'row', split_axis=2, concat_axis=1, tiled=True)  24.7 us
    unnamed x31, local copies, waits for them, and re-layouts  24.6 us
    ppermute x7, waiting for transfers between devices, pairwise_exchange(): done.append(lax.ppermute(sent, axis, [(i, i ^ step) for i in range(size)]))  16.4 us
    ppermute x7, starting transfers between devices, pairwise_exchange(): done.append(lax.ppermute(sent, axis, [(i, i ^ step) for i in range(size)]))  10 us
    all_to_all x1, local copies, waits for them, and re-layouts, local(): lax.all_to_all(packed, 'row', split_axis=2, concat_axis=1, tiled=True)  9.2 us
    all_to_all x1, starting transfers between devices, local(): lax.all_to_all(packed, 'row', split_axis=2, concat_axis=1, tiled=True)  7.28 us
    reshape x1, local copies, waits for them, and re-layouts, local(): packed = flux_y.reshape(planes, owned, 5 * length)  3.7 us
  transfers between devices with their start and end apart: 8, of which 4 were waited for; matrix products, arithmetic and copies ran while one was open for 7% of the time, Pallas kernels for 0%

profile of v1, /device:TPU:0, one launch (start us, length us, event | category | flops | bytes accessed | tf_op | source)
XLA Modules:
  0.0 164.7 jit_solution(4018534087454543467)
XLA Ops:
  0.0 0.0 copy-start
  0.0 1.0 bitcast_dynamic-update-slice_fusion.9
  1.0 0.0 copy-start.2
  1.1 0.0 copy-start.3
  1.1 1.4 multiply_reduce_fusion
  2.5 0.0 copy-done
  2.5 0.0 copy-done.2
  2.5 0.0 copy-done.3
  2.5 0.1 bitcast_dynamic-update-slice_fusion.7
  2.7 3.7 %copy.31 = f32[1,32,5,2048]{1,3,2,0:T(8,128)} copy(f32[1,32,5,2048]{3,1,2,0:T(8,128)S(1)} %bitcast_dynamic-update-slice_fusion.5) | data formatting | bytes 2621440 | tf_op jit(solution)/shard_map/reshape | solution.py:123
  6.4 0.5 broadcast.46
  6.9 47.4 %reduce.1 = f32[10240,32]{1,0:T(8,128)} reduce(f32[10240,1,32]{2,1,0:T(1,128)} %bitcast.135, f32[]{:T(128)} %broadcast.46), dimensions={1}, to_apply=%bitcast.123.reduce_sub_computation | reduce | bytes 2621444
  54.3 5.3 %reshape.167 = f32[8,1,40960]{2,1,0:T(1,128)} reshape(f32[10240,32]{1,0:T(8,128)} %reduce.1) | data formatting | bytes 2621440
  59.6 7.3 %all-to-all-start = ((f32[8,1,40960]{2,1,0:T(1,128)}), f32[8,1,40960]{2,1,0:T(1,128)S(1)}, u32[]{:S(2)}, u32[]{:S(2)}) async-start(f32[8,1,40960]{2,1,0:T(1,128)} %reshape.167), calls=%async_computation | async-start | bytes 2621440 | tf_op jit(solution)/shard_map/all_to_all | solution.py:125
  66.9 0.1 fusion.7
  67.0 0.1 multiply_bitcast_fusion
  67.3 0.0 copy-start.5
  67.5 0.8 copy-done.5
  68.3 3.5 %convolution_bitcast_fusion = f32[5,1,32,16,384]{4,3,2,0,1:T(8,128)S(1)} fusion(f32[5,32,16,128]{3,2,1,0:T(8,128)S(1)} %bitcast_dynamic-update-slice_fusion, f32[128,384,1,1]{1,0,3,2:T(8,128)S(1)} %copy-done.5), kind=kOutput, calls=%fused_computation.1 | convolution fusion | flops 1509949440 | bytes 5439488 | tf_op jit(solution)/shard_map/...bj,jk->...bk/dot_general | solution.py:64
  71.8 0.1 fusion.11
  71.9 0.2 fusion.10
  72.1 1.4 fusion
  73.6 24.7 %all-to-all-done = f32[8,1,40960]{2,1,0:T(1,128)S(1)} async-done(((f32[8,1,40960]{2,1,0:T(1,128)}), f32[8,1,40960]{2,1,0:T(1,128)S(1)}, u32[]{:S(2)}, u32[]{:S(2)}) %all-to-all-start) | async-done | bytes 1310752 | tf_op jit(solution)/shard_map/all_to_all | solution.py:125
  98.3 3.7 %reduce.2 = f32[8,40960]{1,0:T(8,128)S(1)} reduce(f32[8,1,40960]{2,1,0:T(1,128)S(1)} %all-to-all-done, f32[]{:T(128)} %broadcast.46), dimensions={1}, to_apply=%all_to_all.11.reduce_sub_computation | reduce | bytes 2621444 | tf_op jit(solution)/shard_map/all_to_all | solution.py:125
  102.0 10.9 %reshape.168 = f32[10240,1,32]{2,1,0:T(1,128)} reshape(f32[8,40960]{1,0:T(8,128)S(1)} %reduce.2) | data formatting | bytes 2621440
  112.8 9.2 %copy.27 = f32[1,32,10240]{2,1,0:T(8,128)S(1)} copy(f32[1,32,10240]{1,0,2:T(1,128)} %bitcast.136) | data formatting | bytes 2621440 | tf_op jit(solution)/shard_map/all_to_all | solution.py:125
  122.0 0.0 copy-start.4
  122.0 0.2 reshape.152
  122.2 0.7 copy-done.4
  123.0 1.2 fusion.12
  124.2 0.0 copy-start.1
  124.2 0.9 dynamic-slice_bitcast_fusion
  125.1 1.4 collective-permute-start
  126.6 0.0 copy-done.1
  126.6 0.2 reshape.149
  126.8 0.1 collective-permute-start.1
  126.9 2.1 %collective-permute-start.2 = (f32[1,32,1280]{2,1,0:T(8,128)}, f32[1,32,1280]{2,1,0:T(8,128)S(1)}, u32[]{:S(2)}, u32[]{:S(2)}) collective-permute-start(f32[1,32,1280]{2,1,0:T(8,128)} %get-tuple-element.17), channel_id=1, source_target_pairs={{0,12},{4,8},{8,4},{12,0},{16,28},{20,24},{24,20},{28,16},{1,13},{... | collective-permute-start | bytes 491528 | tf_op jit(solution)/shard_map/ppermute | solution.py:25
  128.9 0.2 collective-permute-start.3
  129.2 3.5 %collective-permute-start.4 = (f32[1,32,1280]{2,1,0:T(8,128)S(1)}, f32[1,32,1280]{2,1,0:T(8,128)S(1)}, u32[]{:S(2)}, u32[]{:S(2)}) collective-permute-start(f32[1,32,1280]{2,1,0:T(8,128)S(1)} %get-tuple-element.15), channel_id=1, source_target_pairs={{0,20},{4,16},{8,28},{12,24},{16,4},{20,0},{24,12},{28,8},{1,21},{... | collective-permute-start | bytes 491528 | tf_op jit(solution)/shard_map/ppermute | solution.py:25
  132.7 0.0 collective-permute-done
  132.7 1.5 collective-permute-start.5
  134.2 1.6 bitcast_dynamic-update-slice_fusion.16
  135.8 2.8 %collective-permute-done.1 = f32[1,32,1280]{2,1,0:T(8,128)S(1)} collective-permute-done((f32[1,32,1280]{2,1,0:T(8,128)}, f32[1,32,1280]{2,1,0:T(8,128)S(1)}, u32[]{:S(2)}, u32[]{:S(2)}) %collective-permute-start.1) | collective-permute-done | bytes 163872 | tf_op jit(solution)/shard_map/ppermute | solution.py:25
  138.6 1.2 collective-permute-start.6
  139.8 0.7 bitcast_dynamic-update-slice_fusion.15
  140.5 0.0 collective-permute-done.2
  140.5 0.7 bitcast_dynamic-update-slice_fusion.14
  141.2 9.9 %collective-permute-done.3 = f32[1,32,1280]{2,1,0:T(8,128)S(1)} collective-permute-done((f32[1,32,1280]{2,1,0:T(8,128)S(1)}, f32[1,32,1280]{2,1,0:T(8,128)S(1)}, u32[]{:S(2)}, u32[]{:S(2)}) %collective-permute-start.3) | collective-permute-done | bytes 163872 | tf_op jit(solution)/shard_map/ppermute | solution.py:25
  151.0 0.7 bitcast_dynamic-update-slice_fusion.13
  151.7 3.7 %collective-permute-done.4 = f32[1,32,1280]{2,1,0:T(8,128)S(1)} collective-permute-done((f32[1,32,1280]{2,1,0:T(8,128)S(1)}, f32[1,32,1280]{2,1,0:T(8,128)S(1)}, u32[]{:S(2)}, u32[]{:S(2)}) %collective-permute-start.4) | collective-permute-done | bytes 163872 | tf_op jit(solution)/shard_map/ppermute | solution.py:25
  155.4 0.7 bitcast_dynamic-update-slice_fusion.12
  156.0 0.0 collective-permute-done.5
  156.0 0.7 bitcast_dynamic-update-slice_fusion.11
  156.7 0.0 collective-permute-done.6
  156.7 0.7 bitcast_dynamic-update-slice_fusion.10
  157.4 1.9 %gather_fusion = f32[8,32,1280]{2,1,0:T(8,128)S(1)} fusion(f32[8,32,1280]{2,1,0:T(8,128)} %bitcast.139, s32[1024]{0:T(1024)S(1)} %pad_clamp_fusion), kind=kCustom, calls=%fused_computation | custom fusion | bytes 2621472 | tf_op jit(solution)/shard_map/gather | solution.py:26
  159.4 1.8 %copy.28 = f32[1,32,8,1280]{3,2,1,0:T(8,128)} copy(f32[1,32,8,1280]{3,1,2,0:T(8,128)S(1)} %bitcast.138) | data formatting | bytes 2621440 | tf_op jit(solution)/shard_map/transpose | solution.py:14
  161.2 1.5 reshape_reshape.3
  162.7 2.0 %fusion.1 = f32[5,1,32,2048]{3,2,1,0:T(8,128)} fusion(f32[5,1,32,2048]{3,2,1,0:T(8,128)S(1)} %reshape.149, f32[1,32,5,2048]{3,2,1,0:T(8,128)S(1)} %reshape_reshape.3), kind=kLoop, calls=%fused_computation.5 | loop fusion | flops 655360 | bytes 3932160 | tf_op jit(solution)/shard_map/neg | solution.py:129
  (15 shorter events, 0.5 us)
Async XLA Ops:
  0.0 2.5 %copy-start = (f32[3,1,32,2048]{3,2,1,0:T(8,128)S(1)}, f32[3,1,32,2048]{3,2,1,0:T(8,128)}, u32[]{:S(2)}) copy-start(f32[3,1,32,2048]{3,2,1,0:T(8,128)} %param.6) | copy-start | bytes 2359300
  1.0 1.5 copy-start.2
  1.1 1.5 copy-start.3
  59.6 38.7 %all-to-all-start = ((f32[8,1,40960]{2,1,0:T(1,128)}), f32[8,1,40960]{2,1,0:T(1,128)S(1)}, u32[]{:S(2)}, u32[]{:S(2)}) async-start(f32[8,1,40960]{2,1,0:T(1,128)} %reshape.167), calls=%async_computation | async-start | bytes 2621440 | tf_op jit(solution)/shard_map/all_to_all | solution.py:125
  67.3 0.9 copy-start.5
  122.0 1.0 copy-start.4
  124.2 2.3 %copy-start.1 = (f32[5,1,32,16,128]{4,3,2,0,1:T(8,128)S(1)}, f32[5,1,32,16,128]{4,3,2,0,1:T(8,128)}, u32[]{:S(2)}) copy-start(f32[5,1,32,16,128]{4,3,2,0,1:T(8,128)} %fusion) | copy-start | bytes 3932164
  125.1 7.6 %collective-permute-start = (f32[1,32,1280]{2,1,0:T(8,128)}, f32[1,32,1280]{2,1,0:T(8,128)}, u32[]{:S(2)}, u32[]{:S(2)}) collective-permute-start(f32[1,32,1280]{2,1,0:T(8,128)} %get-tuple-element.19), channel_id=1, source_target_pairs={{0,4},{4,0},{8,12},{12,8},{16,20},{20,16},{24,28},{28,24},{1,5},{5... | collective-permute-start | bytes 491528 | tf_op jit(solution)/shard_map/ppermute | solution.py:25
  126.8 11.8 %collective-permute-start.1 = (f32[1,32,1280]{2,1,0:T(8,128)}, f32[1,32,1280]{2,1,0:T(8,128)S(1)}, u32[]{:S(2)}, u32[]{:S(2)}) collective-permute-start(f32[1,32,1280]{2,1,0:T(8,128)} %get-tuple-element.18), channel_id=1, source_target_pairs={{0,8},{4,12},{8,0},{12,4},{16,24},{20,28},{24,16},{28,20},{1,9},{5... | collective-permute-start | bytes 491528 | tf_op jit(solution)/shard_map/ppermute | solution.py:25
  126.9 13.6 %collective-permute-start.2 = (f32[1,32,1280]{2,1,0:T(8,128)}, f32[1,32,1280]{2,1,0:T(8,128)S(1)}, u32[]{:S(2)}, u32[]{:S(2)}) collective-permute-start(f32[1,32,1280]{2,1,0:T(8,128)} %get-tuple-element.17), channel_id=1, source_target_pairs={{0,12},{4,8},{8,4},{12,0},{16,28},{20,24},{24,20},{28,16},{1,13},{... | collective-permute-start | bytes 491528 | tf_op jit(solution)/shard_map/ppermute | solution.py:25
  128.9 22.1 %collective-permute-start.3 = (f32[1,32,1280]{2,1,0:T(8,128)S(1)}, f32[1,32,1280]{2,1,0:T(8,128)S(1)}, u32[]{:S(2)}, u32[]{:S(2)}) collective-permute-start(f32[1,32,1280]{2,1,0:T(8,128)S(1)} %get-tuple-element.16), channel_id=1, source_target_pairs={{0,16},{4,20},{8,24},{12,28},{16,0},{20,4},{24,8},{28,12},{1,17},{... | collective-permute-start | bytes 491528 | tf_op jit(solution)/shard_map/ppermute | solution.py:25
  129.2 26.2 %collective-permute-start.4 = (f32[1,32,1280]{2,1,0:T(8,128)S(1)}, f32[1,32,1280]{2,1,0:T(8,128)S(1)}, u32[]{:S(2)}, u32[]{:S(2)}) collective-permute-start(f32[1,32,1280]{2,1,0:T(8,128)S(1)} %get-tuple-element.15), channel_id=1, source_target_pairs={{0,20},{4,16},{8,28},{12,24},{16,4},{20,0},{24,12},{28,8},{1,21},{... | collective-permute-start | bytes 491528 | tf_op jit(solution)/shard_map/ppermute | solution.py:25
  132.7 23.3 %collective-permute-start.5 = (f32[1,32,1280]{2,1,0:T(8,128)S(1)}, f32[1,32,1280]{2,1,0:T(8,128)S(1)}, u32[]{:S(2)}, u32[]{:S(2)}) collective-permute-start(f32[1,32,1280]{2,1,0:T(8,128)S(1)} %get-tuple-element.14), channel_id=1, source_target_pairs={{0,24},{4,28},{8,16},{12,20},{16,8},{20,12},{24,0},{28,4},{1,25},{... | collective-permute-start | bytes 491528 | tf_op jit(solution)/shard_map/ppermute | solution.py:25
  138.6 18.1 %collective-permute-start.6 = (f32[1,32,1280]{2,1,0:T(8,128)S(1)}, f32[1,32,1280]{2,1,0:T(8,128)S(1)}, u32[]{:S(2)}, u32[]{:S(2)}) collective-permute-start(f32[1,32,1280]{2,1,0:T(8,128)S(1)} %get-tuple-element.13), channel_id=1, source_target_pairs={{0,28},{4,24},{8,20},{12,16},{16,12},{20,8},{24,4},{28,0},{1,29},{... | collective-permute-start | bytes 491528 | tf_op jit(solution)/shard_map/ppermute | solution.py:25
